TPU v7x, 256 devices: a whole 4x4x8 slice. The times are simulated.
256 devices in a mesh: segment: 2 (over core), ctx: 64 (over x, z, y_hi), tp: 2 (over y_lo).
Axes of the slice: x: 4, y: 4 (y_hi: 2, y_lo: 2; y = y_hi * 2 + y_lo), z: 8, core: 2. Of those that a mesh axis runs over, the one named last changes fastest.
Arguments:
- queries: bfloat16 [8192, 32, 128], P('ctx', 'tp'), may hold values from -14 to 14
- keys: bfloat16 [8192, 8, 128], P('ctx', 'tp'), may hold values from -10 to 10
- values: bfloat16 [8192, 8, 128], P('ctx', 'tp'), may hold values from -6 to 6
- layer_in: bfloat16 [8192, 4096], P('ctx', 'tp'), may hold values from -6 to 6
- w_bc: bfloat16 [1, 4096, 1024], P(None, 'tp'), may hold values from -0.09375 to 0.09375
- w_dt: bfloat16 [1, 4096, 64], P(None, 'tp'), may hold values from -0.09375 to 0.09375
- dt_bias: float32 [1, 64], P(None, 'tp'), may hold values from -1 to 1
- decay_rate: float32 [1, 64], P(None, 'tp'), may hold values from 1.2207031e-05 to 0.06
- skip_gain: float32 [1, 64], P(None, 'tp'), may hold values from 0.5 to 2
- out_gain: float32 [1, 64, 64], P(None, 'tp'), may hold values from 0.5 to 1.5
Outputs:
- section_out: bfloat16 [2, 8192, 4096], P('segment', 'ctx', 'tp')
All inputs are finite; a program needn't handle non-finite values.
Results may differ from a plain program's by a relative error of at most 0.002.
Values may be sent and summed in bfloat16 or wider, within the bound.
No kernel may reach another device: no remote copies, remote signals or barrier semaphores. Data moves between devices by JAX's collectives and lax.ppermute only.
A program may use at most 256 MiB of HBM per device.

v0:
```python
import math

import jax
import jax.numpy as jnp
from jax import lax
from jax.sharding import PartitionSpec as P

GROUPS = 4
STATE = 128


EPSILON = 1e-05


def prefix(part, axis, combine, identity):
    place = lax.axis_index(axis)
    gathered = jax.tree.map(lambda a: lax.all_gather(a, axis), part)
    state = jax.tree.map(lambda a, e: jnp.zeros_like(a) + jnp.asarray(e, a.dtype), part, identity)

    def one(turn, state):
        return combine(
            state, jax.tree.map(lambda a: lax.dynamic_index_in_dim(a, turn, 0, False), gathered)
        )

    return lax.fori_loop(0, place, one, state)


def swapped(value, axis, distance):
    mask = 2**distance
    pairs = [(source, source ^ mask) for source in range(lax.axis_size(axis))]
    return lax.ppermute(value, axis, pairs)


def span_terms(normed, b_rows, c_rows, step_sizes, rate_row, skip_row):
    count_rows, head_count, head_width = normed.shape
    group_count = b_rows.shape[1]
    per_group = head_count // group_count
    state_root = math.sqrt(b_rows.shape[2])
    log_decay = jnp.cumsum(-step_sizes * rate_row[None, :], axis=0)
    lower_mask = jnp.arange(count_rows)[:, None] >= jnp.arange(count_rows)[None, :]
    intersection = (
        jnp.einsum("tgn,sgn->gts", c_rows, b_rows, precision=lax.Precision.HIGHEST) / state_root
    )
    log_gaps = log_decay.T[:, :, None] - log_decay.T[:, None, :]
    decays = jnp.where(lower_mask[None], jnp.exp(jnp.where(lower_mask[None], log_gaps, 0.0)), 0.0)
    mixing = (
        decays.reshape(group_count, per_group, count_rows, count_rows)
        * intersection[:, None]
        * step_sizes.T.reshape(group_count, per_group, 1, count_rows)
    )
    grouped = normed.reshape(count_rows, group_count, per_group, head_width)
    local_part = jnp.einsum(
        "gkts,sgkp->tgkp", mixing, grouped, precision=lax.Precision.HIGHEST
    ).reshape(count_rows, head_count, head_width)
    tail_weight = jnp.exp(log_decay[-1][None, :] - log_decay) * step_sizes
    weighted = (normed * tail_weight[:, :, None]).reshape(
        count_rows, group_count, per_group, head_width
    )
    ending = jnp.einsum(
        "sgkp,sgn->gkpn", weighted, b_rows, precision=lax.Precision.HIGHEST
    ).reshape(head_count, head_width, b_rows.shape[2])
    return (
        log_decay,
        local_part + skip_row[None, :, None] * normed,
        ending,
        jnp.exp(log_decay[-1]),
    )


def span_inflow(log_decay, c_rows, state_in):
    count_rows, group_count, state_n = c_rows.shape
    head_count, head_width = (state_in.shape[0], state_in.shape[1])
    per_group = head_count // group_count
    state_root = math.sqrt(state_n)
    inflow = jnp.einsum(
        "tgn,gkpn->tgkp",
        c_rows,
        state_in.reshape(group_count, per_group, head_width, state_n),
        precision=lax.Precision.HIGHEST,
    )
    return (
        jnp.exp(log_decay)[:, :, None]
        * inflow.reshape(count_rows, head_count, head_width)
        / state_root
    )


def merge_states(earlier, later):
    return (earlier[0] * later[0], later[0][:, None, None] * earlier[1] + later[1])


def body(queries, keys, values, layer_in, w_bc, w_dt, dt_bias, decay_rate, skip_gain, out_gain):
    segment_index = lax.axis_index("segment")
    attention_on = segment_index == 0
    state_on = jnp.logical_not(attention_on)
    row_count, q_heads, head_width = queries.shape
    kv_heads = keys.shape[1]
    group_size = q_heads // kv_heads
    score_scale = 1.0 / math.sqrt(head_width)
    first_row = lax.axis_index("ctx") * row_count
    last_row = first_row + row_count - 1
    query_place = first_row + jnp.arange(row_count, dtype=jnp.int32)
    grouped = queries.reshape(row_count, kv_heads, group_size, head_width).transpose(1, 2, 0, 3)

    def add_block(carried, key_block, value_block, key_start):
        row_top, row_total, row_sum = carried
        scores = (
            jnp.einsum("kgqd,skd->kgqs", grouped, key_block, preferred_element_type=jnp.float32)
            * score_scale
        )
        key_place = key_start + jnp.arange(key_block.shape[0], dtype=jnp.int32)
        allowed = (query_place[:, None] >= key_place[None, :])[None, None]
        masked = jnp.where(allowed, scores, -1e30)
        new_top = jnp.maximum(row_top, jnp.max(masked, axis=3))
        raw_weight = jnp.where(allowed, jnp.exp(masked - new_top[..., None]), 0.0)
        factor = jnp.exp(row_top - new_top)
        new_total = row_total * factor + jnp.sum(raw_weight, axis=3)
        block_sum = jnp.einsum(
            "kgqs,skd->kgqd",
            raw_weight.astype(jnp.bfloat16),
            value_block,
            preferred_element_type=jnp.float32,
        )
        return (new_top, new_total, row_sum * factor[..., None] + block_sum)

    initial = (
        jnp.full((kv_heads, group_size, row_count), -1e30, jnp.float32),
        jnp.zeros((kv_heads, group_size, row_count), jnp.float32),
        jnp.zeros((kv_heads, group_size, row_count, head_width), jnp.float32),
    )
    key_piece = lax.all_gather(keys, "ctx", axis=0, tiled=True)
    value_piece = lax.all_gather(values, "ctx", axis=0, tiled=True)
    key_count = key_piece.shape[0]
    block_size = math.gcd(key_count, 1024)

    def run_all(inner_state):

        def one_step(block_index, loop_state):
            block_start = block_index * block_size
            key_block = lax.dynamic_slice_in_dim(key_piece, block_start, block_size, 0)
            value_block = lax.dynamic_slice_in_dim(value_piece, block_start, block_size, 0)
            return add_block(loop_state, key_block, value_block, block_start)

        return lax.fori_loop(0, key_count // block_size, one_step, inner_state)

    wanted = jnp.logical_and(attention_on, jnp.int32(0) <= last_row)
    row_top, row_total, row_sum = lax.cond(wanted, run_all, lambda kept_state: kept_state, initial)
    safe_total = jnp.where(attention_on, row_total, 1.0)
    mixed_out = row_sum / safe_total[..., None]
    attended = (
        mixed_out.transpose(2, 0, 1, 3)
        .reshape(row_count, q_heads * head_width)
        .astype(jnp.bfloat16)
    )
    current = layer_in
    channel_count = current.shape[1]
    heads_dev = dt_bias.shape[1]
    state_width = channel_count // heads_dev
    groups_dev = GROUPS // lax.axis_size("tp")
    wide_rows = current.astype(jnp.float32)
    part_bc = jnp.dot(current, w_bc[0], preferred_element_type=jnp.float32)
    part_dt = jnp.dot(current, w_dt[0], preferred_element_type=jnp.float32)
    part_sq = jnp.sum(wide_rows * wide_rows, axis=1)
    sum_bc, sum_dt, sum_sq = lax.psum((part_bc, part_dt, part_sq), "tp")
    inv_rms = lax.rsqrt(sum_sq / (channel_count * lax.axis_size("tp")) + EPSILON)
    normed = (wide_rows * inv_rms[:, None]).reshape(row_count, heads_dev, state_width)
    half_cols = GROUPS * STATE
    b_all = sum_bc[:, :half_cols].reshape(row_count, GROUPS, STATE)
    c_all = sum_bc[:, half_cols:].reshape(row_count, GROUPS, STATE)
    group_start = lax.axis_index("tp") * groups_dev
    b_rows = lax.dynamic_slice_in_dim(b_all, group_start, groups_dev, 1) * inv_rms[:, None, None]
    c_rows = lax.dynamic_slice_in_dim(c_all, group_start, groups_dev, 1) * inv_rms[:, None, None]
    own_dt = lax.dynamic_slice_in_dim(sum_dt, lax.axis_index("tp") * heads_dev, heads_dev, 1)
    step_sizes = jax.nn.softplus(own_dt * inv_rms[:, None] + dt_bias[0][None, :])

    def compute_terms(given):
        return span_terms(given[0], given[1], given[2], given[3], decay_rate[0], skip_gain[0])

    def empty_terms(given):
        return (
            jnp.zeros((row_count, heads_dev), jnp.float32),
            jnp.zeros((row_count, heads_dev, state_width), jnp.float32),
            jnp.zeros((heads_dev, state_width, STATE), jnp.float32),
            jnp.zeros((heads_dev,), jnp.float32),
        )

    log_decay, local_part, ending, span_decay = lax.cond(
        state_on, compute_terms, empty_terms, (normed, b_rows, c_rows, step_sizes)
    )
    decay_in, state_in = prefix(
        (span_decay, ending),
        "ctx",
        merge_states,
        (jnp.ones_like(span_decay), jnp.zeros_like(ending)),
    )
    mixed_out = local_part + span_inflow(log_decay, c_rows, state_in)
    power = jnp.mean(mixed_out * mixed_out, axis=2, keepdims=True)
    result = wide_rows.reshape(row_count, heads_dev, state_width) + out_gain[0][
        None
    ] * mixed_out * lax.rsqrt(power + EPSILON)
    current = result.reshape(row_count, channel_count).astype(jnp.bfloat16)
    result = jnp.where(attention_on, attended, current)
    incoming = swapped(result, "segment", 0)
    return incoming[None]


def solution(mesh):
    in_specs = (
        P("ctx", "tp", None),
        P("ctx", "tp", None),
        P("ctx", "tp", None),
        P("ctx", "tp"),
        P(None, "tp", None),
        P(None, "tp", None),
        P(None, "tp"),
        P(None, "tp"),
        P(None, "tp"),
        P(None, "tp", None),
    )
    out_specs = P("segment", "ctx", "tp")
    return jax.shard_map(body, mesh=mesh, in_specs=in_specs, out_specs=out_specs, check_vma=False)
```

profile of v0, /device:TPU:231, one launch (start us, length us, event | category | flops | bytes accessed | tf_op | source)
XLA Modules:
  0.0 1026.7 jit_solution(16598531643501486196)
XLA Ops:
  7.4 3.9 fusion.43
  11.4 1.6 copy.52
  13.1 1.6 copy.54
  16.7 6.5 all-reduce.1
  23.3 28.8 %all-reduce.4.cloned.1.call-done = f32[128,1024]{1,0:T(8,128)} async-done(((f32[128,1024]{1,0:T(8,128)}), f32[128,1024]{1,0:T(8,128)}) %all-reduce.4.cloned.1.call-update) | async-done | bytes 524304 | tf_op jit(solution)/shard_map/psum | solution.py:164
  54.0 19.6 %conditional.3 = (f32[128,32]{1,0:T(8,128)}, f32[128,32,64]{0,2,1:T(8,128)S(1)}, f32[32,64,128]{2,1,0:T(8,128)}, f32[32]{0:T(128)}) conditional(s32[]{:T(128)} %convert_element_type.36, () %tuple.55, (s32[]{:T(128)}, f32[128,64]{0,1:T(8,128)S(1)}, f32[128]{0:T(128)S(1)}, f32[1,32]{1,0:T(1,128)S(1)}, f32[1,32]{1,0:T(1,128)S(1)}, ...), branch_computations={%region_10.11_spmd, %region_11.13_spmd} | conditional | flops 860024832 | bytes 13620502 | solution.py:187
  55.7 1.6 exponential_multiply_fusion
  57.3 1.5 copy.45
  62.4 5.2 fusion
  69.4 3.1 fusion.8
  77.8 152.6 %all-reduce = f32[2048]{0:T(1024)S(1)} all-reduce(f32[2048]{0:T(1024)S(1)} %dynamic-update-slice), channel_id=2, replica_groups=mesh['segment'=2,'ctx'=64,'tp'=2] {'ctx'}, use_global_device_ids=true, to_apply=%add | all-reduce | flops 2048 | bytes 16384
  231.9 73.6 %all-gather.8.cloned.1.call-done = bf16[8192,4,128]{2,0,1:T(8,128)(2,1)} async-done(((bf16[128,4,128]{2,0,1:T(8,128)(2,1)}), bf16[8192,4,128]{2,0,1:T(8,128)(2,1)}) %all-gather.8.cloned.1.call-update) | async-done | bytes 8388624 | tf_op jit(solution)/shard_map/all_gather | solution.py:132
  305.5 1.7 conditional.2
  307.2 1.6 fusion.47
  309.8 568.6 %all-gather.10.cloned.1.call-done = f32[2048,64,128]{2,1,0:T(8,128)} async-done(((f32[32,64,128]{2,1,0:T(8,128)}), f32[2048,64,128]{2,1,0:T(8,128)}) %all-gather.10.cloned.1.call-update) | async-done | bytes 67108880 | tf_op jit(solution)/shard_map/all_gather | solution.py:17
  878.5 133.8 %while.30 = (s32[]{:T(128)}, f32[32,64,128]{2,1,0:T(8,128)S(1)}, s32[]{:T(128)}, f32[64,32]{1,0:T(8,128)}, f32[64,32,64,128]{3,2,1,0:T(8,128)}, /*index=5*/s32[]{:T(128)}, s32[]{:T(128)}, s32[]{:T(128)}) while((s32[]{:T(128)}, f32[32,64,128]{2,1,0:T(8,128)S(1)}, s32[]{:T(128)}, f32[64,32]{1,0:T(8,128)}, f32[64,32,64,128]{3,2,1,0:T(8,128)}, ...), condition=%wide.region_14.15_spmd, body=%wide.region_13.14_spmd.sunk | while | flops 524293 | bytes 3146239 | solution.py:25
  881.4 1.4 bitcast_add_fusion.3
  885.7 1.4 bitcast_add_fusion.3
  890.0 1.4 bitcast_add_fusion.3
  894.3 1.4 bitcast_add_fusion.3
  905.1 1.4 bitcast_add_fusion.3
  907.3 1.4 bitcast_add_fusion.3
  909.4 1.4 bitcast_add_fusion.3
  918.1 1.4 bitcast_add_fusion.3
  920.2 1.4 bitcast_add_fusion.3
  928.9 1.4 bitcast_add_fusion.3
  933.2 1.4 bitcast_add_fusion.3
  939.7 1.4 bitcast_add_fusion.3
  944.0 1.4 bitcast_add_fusion.3
  948.3 1.4 bitcast_add_fusion.3
  1015.0 1.5 collective-permute-start
  1016.5 1.5 collective-permute-done
  (176 shorter events, 135.3 us)
Async XLA Ops:
  7.4 9.1 copy-start
  7.4 9.1 copy-start.2
  7.4 46.6 %copy-start.6 = (f32[1,32]{1,0:T(1,128)S(1)}, f32[1,32]{1,0:T(1,128)}, u32[]{:S(2)}) copy-start(f32[1,32]{1,0:T(1,128)} %param.24) | copy-start | bytes 388
  7.4 46.6 %copy-start.7 = (f32[1,32]{1,0:T(1,128)S(1)}, f32[1,32]{1,0:T(1,128)}, u32[]{:S(2)}) copy-start(f32[1,32]{1,0:T(1,128)} %param.25) | copy-start | bytes 388
  7.4 44.7 %all-reduce.4.cloned.1.call-start = ((), (), s32[]{:S(2)}) async-start(), calls=%async_computation.2 | async-start | bytes 1048576 | tf_op jit(solution)/shard_map/psum | solution.py:164
  11.4 220.6 %all-gather.6.cloned.1.call-start = ((), (), s32[]{:S(2)}) async-start(), calls=%async_computation | async-start | bytes 8519680 | tf_op jit(solution)/shard_map/all_gather | solution.py:131
  13.0 292.5 %all-gather.8.cloned.1.call-start = ((), (), s32[]{:S(2)}) async-start(), calls=%async_computation.1 | async-start | bytes 8519680 | tf_op jit(solution)/shard_map/all_gather | solution.py:132
  14.7 863.7 %all-gather.10.cloned.1.call-start = ((), (), s32[]{:S(2)}) async-start(), calls=%async_computation.3 | async-start | bytes 68157440 | tf_op jit(solution)/shard_map/all_gather | solution.py:17
  54.0 4.9 copy-start.5
  60.9 6.8 copy-start.4
  1012.4 2.5 copy-start.3
  1015.0 3.1 collective-permute-start
Sparse Core Ops, SparseCore 0:
  11.5 40.5 all-reduce.3
Sparse Core Ops, SparseCore 1:
  15.4 144.2 all-gather.5
  163.0 142.4 all-gather.7
  308.9 569.5 all-gather.9
where the time goes:
time: 1030 us
  waiting for transfers between devices  673 us (65%)
  blocking collectives  159 us (15%)
  other arithmetic  96.8 us (9%)
  local copies, waits for them, and re-layouts  63.5 us (6%)
  between operations  15.9 us (2%)
  matrix products  14.9 us (1%)
    all_gather x1, waiting for transfers between devices, prefix(): gathered = jax.tree.map(lambda a: lax.all_gather(a, axis), part)  569 us
    unnamed x1, blocking collectives  153 us
    add x62, other arithmetic, merge_states(): later[0][:, None, None] * earlier[1] + later[1]  89.2 us
    all_gather x1, waiting for transfers between devices, body(): value_piece = lax.all_gather(values, 'ctx', axis=0, tiled=True)  73.6 us
    mul x62, local copies, waits for them, and re-layouts, merge_states(): later[0][:, None, None] * earlier[1] + later[1]  42.6 us
    psum x1, waiting for transfers between devices, body(): sum_bc, sum_dt, sum_sq = lax.psum((part_bc, part_dt, part_sq), 'tp')  28.8 us
  transfers between devices with their start and end apart: 5, of which 4 were waited for; matrix products, arithmetic and copies ran while one was open for 3% of the time, Pallas kernels for 0%

commit v1 on v0

v1 whole, which is shorter than its diff:
```python
import math

import jax
import jax.numpy as jnp
from jax import lax
from jax.sharding import PartitionSpec as P

GROUPS = 4
STATE = 128


EPSILON = 1e-05


def shifted_up(value, axis, distance):
    size = lax.axis_size(axis)
    pairs = [(source, source + distance) for source in range(size - distance)]
    return lax.ppermute(value, axis, pairs)


def swapped(value, axis):
    return lax.ppermute(value, axis, [(0, 1), (1, 0)])


def span_terms(normed, b_rows, c_rows, step_sizes, rate_row, skip_row):
    count_rows, head_count, head_width = normed.shape
    group_count = b_rows.shape[1]
    per_group = head_count // group_count
    state_root = math.sqrt(b_rows.shape[2])
    log_decay = jnp.cumsum(-step_sizes * rate_row[None, :], axis=0)
    lower_mask = jnp.arange(count_rows)[:, None] >= jnp.arange(count_rows)[None, :]
    intersection = (
        jnp.einsum("tgn,sgn->gts", c_rows, b_rows, precision=lax.Precision.HIGHEST) / state_root
    )
    log_gaps = log_decay.T[:, :, None] - log_decay.T[:, None, :]
    decays = jnp.where(lower_mask[None], jnp.exp(jnp.where(lower_mask[None], log_gaps, 0.0)), 0.0)
    mixing = (
        decays.reshape(group_count, per_group, count_rows, count_rows)
        * intersection[:, None]
        * step_sizes.T.reshape(group_count, per_group, 1, count_rows)
    )
    grouped = normed.reshape(count_rows, group_count, per_group, head_width)
    local_part = jnp.einsum(
        "gkts,sgkp->tgkp", mixing, grouped, precision=lax.Precision.HIGHEST
    ).reshape(count_rows, head_count, head_width)
    tail_weight = jnp.exp(log_decay[-1][None, :] - log_decay) * step_sizes
    weighted = (normed * tail_weight[:, :, None]).reshape(
        count_rows, group_count, per_group, head_width
    )
    ending = jnp.einsum(
        "sgkp,sgn->gkpn", weighted, b_rows, precision=lax.Precision.HIGHEST
    ).reshape(head_count, head_width, b_rows.shape[2])
    return (
        log_decay,
        local_part + skip_row[None, :, None] * normed,
        ending,
        jnp.exp(log_decay[-1]),
    )


def span_inflow(log_decay, c_rows, state_in):
    count_rows, group_count, state_n = c_rows.shape
    head_count, head_width = (state_in.shape[0], state_in.shape[1])
    per_group = head_count // group_count
    state_root = math.sqrt(state_n)
    inflow = jnp.einsum(
        "tgn,gkpn->tgkp",
        c_rows,
        state_in.reshape(group_count, per_group, head_width, state_n),
        precision=lax.Precision.HIGHEST,
    )
    return (
        jnp.exp(log_decay)[:, :, None]
        * inflow.reshape(count_rows, head_count, head_width)
        / state_root
    )


def merge_states(earlier, later):
    return (earlier[0] * later[0], later[0][:, None, None] * earlier[1] + later[1])


def exclusive_scan(decay, state, axis):
    place = lax.axis_index(axis)
    size = lax.axis_size(axis)
    incl = (decay, state)
    excl = (jnp.ones_like(decay), jnp.zeros_like(state))
    distance = 1
    while distance < size:
        got = jax.tree.map(lambda a: shifted_up(a, axis, distance), incl)
        present = place >= distance
        got = (jnp.where(present, got[0], 1.0), jnp.where(present, got[1], 0.0))
        excl = merge_states(got, excl)
        if distance * 2 < size:
            incl = merge_states(got, incl)
        distance *= 2
    return excl


def attention_half(queries, keys, values, first_row):
    row_count, q_heads, head_width = queries.shape
    kv_heads = keys.shape[1]
    group_size = q_heads // kv_heads
    score_scale = 1.0 / math.sqrt(head_width)
    last_row = first_row + row_count - 1
    query_place = first_row + jnp.arange(row_count, dtype=jnp.int32)
    grouped = queries.reshape(row_count, kv_heads, group_size, head_width).transpose(1, 2, 0, 3)
    both = jnp.concatenate([keys, values], axis=1)
    both_all = lax.all_gather(both, "ctx", axis=0, tiled=True)
    key_count = both_all.shape[0]
    block_size = math.gcd(key_count, 1024)

    def add_block(block_index, carried):
        row_top, row_total, row_sum = carried
        block_start = block_index * block_size
        block = lax.dynamic_slice_in_dim(both_all, block_start, block_size, 0)
        key_block = block[:, :kv_heads]
        value_block = block[:, kv_heads:]
        scores = (
            jnp.einsum("kgqd,skd->kgqs", grouped, key_block, preferred_element_type=jnp.float32)
            * score_scale
        )
        key_place = block_start + jnp.arange(block_size, dtype=jnp.int32)
        allowed = (query_place[:, None] >= key_place[None, :])[None, None]
        masked = jnp.where(allowed, scores, -1e30)
        new_top = jnp.maximum(row_top, jnp.max(masked, axis=3))
        raw_weight = jnp.where(allowed, jnp.exp(masked - new_top[..., None]), 0.0)
        factor = jnp.exp(row_top - new_top)
        new_total = row_total * factor + jnp.sum(raw_weight, axis=3)
        block_sum = jnp.einsum(
            "kgqs,skd->kgqd",
            raw_weight.astype(jnp.bfloat16),
            value_block,
            preferred_element_type=jnp.float32,
        )
        return (new_top, new_total, row_sum * factor[..., None] + block_sum)

    initial = (
        jnp.full((kv_heads, group_size, row_count), -1e30, jnp.float32),
        jnp.zeros((kv_heads, group_size, row_count), jnp.float32),
        jnp.zeros((kv_heads, group_size, row_count, head_width), jnp.float32),
    )
    block_count = last_row // block_size + 1
    row_top, row_total, row_sum = lax.fori_loop(0, block_count, add_block, initial)
    mixed_out = row_sum / row_total[..., None]
    return (
        mixed_out.transpose(2, 0, 1, 3)
        .reshape(row_count, q_heads * head_width)
        .astype(jnp.bfloat16)
    )


def body(queries, keys, values, layer_in, w_bc, w_dt, dt_bias, decay_rate, skip_gain, out_gain):
    seg = lax.axis_index("segment")
    seg_count = lax.axis_size("segment")
    tp = lax.axis_index("tp")
    tp_count = lax.axis_size("tp")
    row_count, q_heads, head_width = queries.shape
    kv_heads = keys.shape[1]
    first_row = lax.axis_index("ctx") * row_count

    q_share = q_heads // seg_count
    kv_share = kv_heads // seg_count
    q_part = lax.dynamic_slice_in_dim(queries, seg * q_share, q_share, 1)
    k_part = lax.dynamic_slice_in_dim(keys, seg * kv_share, kv_share, 1)
    v_part = lax.dynamic_slice_in_dim(values, seg * kv_share, kv_share, 1)
    attended = attention_half(q_part, k_part, v_part, first_row)

    current = layer_in
    channel_count = current.shape[1]
    heads_dev = dt_bias.shape[1]
    state_width = channel_count // heads_dev
    groups_dev = GROUPS // tp_count
    groups_core = groups_dev // seg_count
    heads_core = heads_dev // seg_count
    half_cols = GROUPS * STATE
    wide_rows = current.astype(jnp.float32)
    part_bc = jnp.dot(current, w_bc[0], preferred_element_type=jnp.float32)
    part_dt = jnp.dot(current, w_dt[0], preferred_element_type=jnp.float32)
    part_sq = jnp.sum(wide_rows * wide_rows, axis=1)

    def columns_for(tp_index):
        group_start = (tp_index * groups_dev + seg * groups_core) * STATE
        head_start = tp_index * heads_dev + seg * heads_core
        return jnp.concatenate(
            [
                lax.dynamic_slice_in_dim(part_bc, group_start, groups_core * STATE, 1),
                lax.dynamic_slice_in_dim(part_bc, half_cols + group_start, groups_core * STATE, 1),
                lax.dynamic_slice_in_dim(part_dt, head_start, heads_core, 1),
                part_sq[:, None],
            ],
            axis=1,
        )

    mine = columns_for(tp)
    theirs = columns_for(tp_count - 1 - tp)
    total = mine + swapped(theirs, "tp")
    width_bc = groups_core * STATE
    sum_b = total[:, :width_bc]
    sum_c = total[:, width_bc : 2 * width_bc]
    sum_dt = total[:, 2 * width_bc : 2 * width_bc + heads_core]
    sum_sq = total[:, 2 * width_bc + heads_core]
    inv_rms = lax.rsqrt(sum_sq / (channel_count * tp_count) + EPSILON)
    own_rows = lax.dynamic_slice_in_dim(wide_rows, seg * heads_core * state_width, heads_core * state_width, 1)
    normed = (own_rows * inv_rms[:, None]).reshape(row_count, heads_core, state_width)
    b_rows = (sum_b * inv_rms[:, None]).reshape(row_count, groups_core, STATE)
    c_rows = (sum_c * inv_rms[:, None]).reshape(row_count, groups_core, STATE)
    bias = lax.dynamic_slice_in_dim(dt_bias[0], seg * heads_core, heads_core, 0)
    rate = lax.dynamic_slice_in_dim(decay_rate[0], seg * heads_core, heads_core, 0)
    skip = lax.dynamic_slice_in_dim(skip_gain[0], seg * heads_core, heads_core, 0)
    gain = lax.dynamic_slice_in_dim(out_gain[0], seg * heads_core, heads_core, 0)
    step_sizes = jax.nn.softplus(sum_dt * inv_rms[:, None] + bias[None, :])

    log_decay, local_part, ending, span_decay = span_terms(
        normed, b_rows, c_rows, step_sizes, rate, skip
    )
    _, state_in = exclusive_scan(span_decay, ending, "ctx")
    mixed_out = local_part + span_inflow(log_decay, c_rows, state_in)
    power = jnp.mean(mixed_out * mixed_out, axis=2, keepdims=True)
    result = own_rows.reshape(row_count, heads_core, state_width) + gain[None] * mixed_out * lax.rsqrt(
        power + EPSILON
    )
    state_part = result.reshape(row_count, heads_core * state_width).astype(jnp.bfloat16)

    keep_state = seg == 0
    outgoing = jnp.where(keep_state, attended, state_part)
    incoming = swapped(outgoing, "segment")
    first = jnp.where(keep_state, state_part, incoming)
    second = jnp.where(keep_state, incoming, attended)
    return jnp.concatenate([first, second], axis=1)[None]


def solution(mesh):
    in_specs = (
        P("ctx", "tp", None),
        P("ctx", "tp", None),
        P("ctx", "tp", None),
        P("ctx", "tp"),
        P(None, "tp", None),
        P(None, "tp", None),
        P(None, "tp"),
        P(None, "tp"),
        P(None, "tp"),
        P(None, "tp", None),
    )
    out_specs = P("segment", "ctx", "tp")
    return jax.shard_map(body, mesh=mesh, in_specs=in_specs, out_specs=out_specs, check_vma=False)
```

time: 1030 us -> 274 us (0.27)
  waiting for transfers between devices: 673 us -> 122 us
  blocking collectives: 159 us -> 0 us
  other arithmetic: 96.8 us -> 25.7 us
  matrix products: 14.9 us -> 58.2 us
  local copies, waits for them, and re-layouts: 63.5 us -> 29.4 us
  starting transfers between devices: 1.71 us -> 21.3 us
    all_gather x3 -> x1, waiting for transfers between devices: 642 us -> 20.6 us  [attention_half(): both_all = lax.all_gather(both, 'ctx', axis=0, tiled=True)]
    unnamed x1 -> x0, blocking collectives: 153 us -> none
    ppermute x1 -> x13, waiting for transfers between devices: 1.54 us -> 101 us  [the longest x11 96.9 us: shifted_up(): return lax.ppermute(value, axis, pairs)]
    add x62 -> x5, other arithmetic: 89.2 us -> 6.94 us  [merge_states(): later[0][:, None, None] * earlier[1] + later[1]]
    dot_general x0 -> x16, matrix products: none -> 45.4 us  [the longest x8 30.9 us: add_block(): jnp.einsum('kgqs,skd->kgqd', raw_weight.astype(jnp.bfloat16), value_block...]
    mul x64 -> x5, local copies, waits for them, and re-layouts: 44.1 us -> 4.21 us  [the longest x3 2.75 us: span_terms(): skip_row[None, :, None] * normed]
    psum x1 -> x0, waiting for transfers between devices: 28.8 us -> none  [body(): sum_bc, sum_dt, sum_sq = lax.psum((part_bc, part_dt, part_sq), 'tp')]
    ppermute x1 -> x13, starting transfers between devices: 1.54 us -> 21.3 us  [the longest x11 18.5 us: shifted_up(): return lax.ppermute(value, axis, pairs)]
  transfers between devices with their start and end apart: 5 -> 14, of which waited for: 4 -> 13; matrix products, arithmetic and copies ran while one was open for 3% -> 13% of each run, Pallas kernels for 0% -> 0%
where the time goes in v1:
time: 274 us; the launch traced here: 271 us
  waiting for transfers between devices  122 us (45%)
  matrix products  58.2 us (21%)
  local copies, waits for them, and re-layouts  29.4 us (11%)
  other arithmetic  25.7 us (9%)
  starting transfers between devices  21.3 us (8%)
  between operations  13.8 us (5%)
    ppermute x11, waiting for transfers between devices, shifted_up(): return lax.ppermute(value, axis, pairs)  96.9 us
    dot_general x8, matrix products, add_block(): jnp.einsum('kgqs,skd->kgqd', raw_weight.astype(jnp.bfloat16), value_block...  30.9 us
    all_gather x1, waiting for transfers between devices, attention_half(): both_all = lax.all_gather(both, 'ctx', axis=0, tiled=True)  20.6 us
    ppermute x11, starting transfers between devices, shifted_up(): return lax.ppermute(value, axis, pairs)  18.5 us
    while x24, local copies, waits for them, and re-layouts  15.9 us
    dot_general x8, matrix products, add_block(): jnp.einsum('kgqd,skd->kgqs', grouped, key_block, preferred_element_type=j...  14.5 us
    reduce_sum x8, other arithmetic, add_block(): new_total = row_total * factor + jnp.sum(raw_weight, axis=3)  8.18 us
    add x5, other arithmetic, merge_states(): later[0][:, None, None] * earlier[1] + later[1]  6.94 us
  transfers between devices with their start and end apart: 14, of which 13 were waited for; matrix products, arithmetic and copies ran while one was open for 13% of the time, Pallas kernels for 0%

profile of v1, /device:TPU:231, one launch (start us, length us, event | category | flops | bytes accessed | tf_op | source)
XLA Modules:
  0.0 271.3 jit_solution(10316998573162825746)
XLA Ops:
  11.2 4.1 %fusion.17 = f32[128,1024]{0,1:T(8,128)S(1)} fusion(bf16[128,2048]{1,0:T(8,128)(2,1)} %param.15, bf16[1,2048,1024]{2,1,0:T(8,128)(2,1)} %param.16), kind=kOutput, calls=%fused_computation.22 | convolution fusion | flops 536870912 | bytes 5242880 | tf_op jit(solution)/shard_map/dot_general | solution.py:178
  17.2 3.2 %collective-permute-done = f32[128,273]{0,1:T(8,128)S(1)} collective-permute-done((f32[128,273]{0,1:T(8,128)S(1)}, f32[128,273]{0,1:T(8,128)S(1)}, u32[]{:S(2)}, u32[]{:S(2)}) %collective-permute-start) | collective-permute-done | bytes 139808 | tf_op jit(solution)/shard_map/ppermute | solution.py:22
  22.2 4.8 %collective-permute-start.6 = (f32[16,64,128]{2,1,0:T(8,128)S(1)}, f32[16,64,128]{2,1,0:T(8,128)}, u32[]{:S(2)}, u32[]{:S(2)}) collective-permute-start(f32[16,64,128]{2,1,0:T(8,128)S(1)} %fusion.76), channel_id=1, source_target_pairs={{0,2},{2,4},{4,6},{6,8},{8,10},{10,12},{12,14},{14,16},{16,18},{18... | collective-permute-start | bytes 1572872 | tf_op jit(solution)/shard_map/ppermute | solution.py:18
  27.1 13.7 %collective-permute-done.6 = f32[16,64,128]{2,1,0:T(8,128)} collective-permute-done((f32[16,64,128]{2,1,0:T(8,128)S(1)}, f32[16,64,128]{2,1,0:T(8,128)}, u32[]{:S(2)}, u32[]{:S(2)}) %collective-permute-start.6) | collective-permute-done | bytes 524320 | tf_op jit(solution)/shard_map/ppermute | solution.py:18
  45.2 9.8 %collective-permute-done.1 = f32[16]{0:T(128)S(1)} collective-permute-done((f32[16]{0:T(128)S(1)}, f32[16]{0:T(128)S(1)}, u32[]{:S(2)}, u32[]{:S(2)}) %collective-permute-start.1) | collective-permute-done | bytes 96 | tf_op jit(solution)/shard_map/ppermute | solution.py:18
  60.7 3.5 %collective-permute-done.2 = f32[16]{0:T(128)S(1)} collective-permute-done((f32[16]{0:T(128)}, f32[16]{0:T(128)S(1)}, u32[]{:S(2)}, u32[]{:S(2)}) %collective-permute-start.2) | collective-permute-done | bytes 96 | tf_op jit(solution)/shard_map/ppermute | solution.py:18
  64.8 24.8 %collective-permute-done.8 = f32[16,64,128]{2,1,0:T(8,128)S(1)} collective-permute-done((f32[16,64,128]{2,1,0:T(8,128)S(1)}, f32[16,64,128]{2,1,0:T(8,128)S(1)}, u32[]{:S(2)}, u32[]{:S(2)}) %collective-permute-start.8) | collective-permute-done | bytes 524320 | tf_op jit(solution)/shard_map/ppermute | solution.py:18
  93.7 5.5 %collective-permute-done.3 = f32[16]{0:T(128)S(1)} collective-permute-done((f32[16]{0:T(128)}, f32[16]{0:T(128)S(1)}, u32[]{:S(2)}, u32[]{:S(2)}) %collective-permute-start.3) | collective-permute-done | bytes 96 | tf_op jit(solution)/shard_map/ppermute | solution.py:18
  99.9 8.4 %collective-permute-done.9 = f32[16,64,128]{2,1,0:T(8,128)} collective-permute-done((f32[16,64,128]{2,1,0:T(8,128)S(1)}, f32[16,64,128]{2,1,0:T(8,128)}, u32[]{:S(2)}, u32[]{:S(2)}) %collective-permute-start.9) | collective-permute-done | bytes 524320 | tf_op jit(solution)/shard_map/ppermute | solution.py:18
  118.6 9.1 %collective-permute-done.4 = f32[16]{0:T(128)} collective-permute-done((f32[16]{0:T(128)}, f32[16]{0:T(128)}, u32[]{:S(2)}, u32[]{:S(2)}) %collective-permute-start.4) | collective-permute-done | bytes 96 | tf_op jit(solution)/shard_map/ppermute | solution.py:18
  128.4 2.1 multiply_add_fusion.1
  133.9 3.0 %fusion.19 = f32[16,64,128]{2,1,0:T(8,128)S(1)} fusion(f32[128,16,64]{0,2,1:T(8,128)S(1)} %bitcast.158, f32[16,128]{1,0:T(8,128)} %get-tuple-element.107, f32[128,128]{1,0:T(8,128)S(1)} %convolution_multiply_fusion, f32[16,128]{1,0:T(8,128)S(1)} %copy.52, pred[128,128]{1,0:T(8,128)(4,1)} %iota_compare_fusion), kind=kOutput, calls=%fused_computation.25 | convolution fusion | flops 202637312 | bytes 1146880 | tf_op jit(solution)/shard_map/gkts,sgkp->tgkp/dot_general | solution.py:43
  138.2 15.2 %collective-permute-done.5 = f32[16]{0:T(128)S(1)} collective-permute-done((f32[16]{0:T(128)}, f32[16]{0:T(128)S(1)}, u32[]{:S(2)}, u32[]{:S(2)}) %collective-permute-start.5) | collective-permute-done | bytes 96 | tf_op jit(solution)/shard_map/ppermute | solution.py:18
  154.0 6.3 %collective-permute-done.11 = f32[16,64,128]{2,1,0:T(8,128)} collective-permute-done((f32[16,64,128]{2,1,0:T(8,128)}, f32[16,64,128]{2,1,0:T(8,128)}, u32[]{:S(2)}, u32[]{:S(2)}) %collective-permute-start.11) | collective-permute-done | bytes 524320 | tf_op jit(solution)/shard_map/ppermute | solution.py:18
  160.3 3.5 %fusion.29 = (f32[128,16]{0,1:T(8,128)S(1)}, f32[16,64,128]{2,1,0:T(8,128)}) fusion(f32[16,64,128]{2,1,0:T(8,128)S(1)} %fusion.19, f32[16]{0:T(128)} %copy-done.14, f32[128,16]{0,1:T(8,128)S(1)} %copy.54, f32[128,1024]{0,1:T(8,128)S(1)} %get-tuple-element.98, f32[128,273]{0,1:T(8,128)} %copy-done.6, f32[128]{0:T(128)S(1)} %fusion.88, ...), kind=kOutput, calls=%fused_computation.38 | convolution fusion | flops 204355584 | bytes 4802310 | tf_op jit(solution)/shard_map/tgn,gkpn->tgkp/dot_general | solution.py:66
  164.3 20.6 %all-gather.2.cloned.1.call-done = bf16[8192,4,128]{2,0,1:T(8,128)(2,1)} async-done(((bf16[128,4,128]{2,0,1:T(8,128)(2,1)}), bf16[8192,4,128]{2,0,1:T(8,128)(2,1)}) %all-gather.2.cloned.1.call-update) | async-done | bytes 8388624 | tf_op jit(solution)/shard_map/all_gather | solution.py:109
  185.0 72.2 %while.15 = (s32[]{:T(128)}, f32[2,4,128]{2,1,0:T(4,128)S(1)}, f32[2,4,128]{2,1,0:T(4,128)S(1)}, f32[2,4,128,128]{3,2,1,0:T(8,128)S(1)}, s32[]{:T(128)}, /*index...) while((s32[]{:T(128)}, f32[2,4,128]{2,1,0:T(4,128)S(1)}, ...), condition=%wide.region_6.7_spmd.clone, body=%wide.region_3.6_spmd.clone.sunk | while | flops 550898816 | bytes 32318704 | solution.py:144
  187.3 2.0 copy-done.1
  190.4 3.9 %fusion.118 = f32[2,4,128,128]{3,2,1,0:T(8,128)S(1)} fusion(f32[2,1024,4,128]{3,1,2,0:T(8,128)} %copy-done.1, f32[2,4,128]{2,1,0:T(4,128)S(1)} %max.29, pred[128,1024]{0,1:T(8,128)(4,1)S(1)} %broadcast_compare_fusion.2, bf16[8192,4,128]{2,0,1:T(8,128)(2,1)} %get-tuple-element.210, s32[]{:T(128)S(6)} %select_n.373, s32[]{:T(128)S(6)} %add.345, ...), kind=kOutput, calls=%fused_computation.8.clone.1 | convolution fusion | flops 273940480 | bytes 5906440 | tf_op jit(solution)/shard_map/while/body/kgqs,skd->kgqd/dot_general | solution.py:130
  199.4 3.9 %fusion.118 = f32[2,4,128,128]{3,2,1,0:T(8,128)S(1)} fusion(f32[2,1024,4,128]{3,1,2,0:T(8,128)} %copy-done.1, f32[2,4,128]{2,1,0:T(4,128)S(1)} %max.29, pred[128,1024]{0,1:T(8,128)(4,1)S(1)} %broadcast_compare_fusion.2, bf16[8192,4,128]{2,0,1:T(8,128)(2,1)} %get-tuple-element.210, s32[]{:T(128)S(6)} %select_n.373, s32[]{:T(128)S(6)} %add.345, ...), kind=kOutput, calls=%fused_computation.8.clone.1 | convolution fusion | flops 273940480 | bytes 5906440 | tf_op jit(solution)/shard_map/while/body/kgqs,skd->kgqd/dot_general | solution.py:130
  205.3 2.0 copy-done.1
  208.4 3.9 %fusion.118 = f32[2,4,128,128]{3,2,1,0:T(8,128)S(1)} fusion(f32[2,1024,4,128]{3,1,2,0:T(8,128)} %copy-done.1, f32[2,4,128]{2,1,0:T(4,128)S(1)} %max.29, pred[128,1024]{0,1:T(8,128)(4,1)S(1)} %broadcast_compare_fusion.2, bf16[8192,4,128]{2,0,1:T(8,128)(2,1)} %get-tuple-element.210, s32[]{:T(128)S(6)} %select_n.373, s32[]{:T(128)S(6)} %add.345, ...), kind=kOutput, calls=%fused_computation.8.clone.1 | convolution fusion | flops 273940480 | bytes 5906440 | tf_op jit(solution)/shard_map/while/body/kgqs,skd->kgqd/dot_general | solution.py:130
  214.3 2.0 copy-done.1
  217.4 3.9 %fusion.118 = f32[2,4,128,128]{3,2,1,0:T(8,128)S(1)} fusion(f32[2,1024,4,128]{3,1,2,0:T(8,128)} %copy-done.1, f32[2,4,128]{2,1,0:T(4,128)S(1)} %max.29, pred[128,1024]{0,1:T(8,128)(4,1)S(1)} %broadcast_compare_fusion.2, bf16[8192,4,128]{2,0,1:T(8,128)(2,1)} %get-tuple-element.210, s32[]{:T(128)S(6)} %select_n.373, s32[]{:T(128)S(6)} %add.345, ...), kind=kOutput, calls=%fused_computation.8.clone.1 | convolution fusion | flops 273940480 | bytes 5906440 | tf_op jit(solution)/shard_map/while/body/kgqs,skd->kgqd/dot_general | solution.py:130
  223.3 2.0 copy-done.1
  226.4 3.9 %fusion.118 = f32[2,4,128,128]{3,2,1,0:T(8,128)S(1)} fusion(f32[2,1024,4,128]{3,1,2,0:T(8,128)} %copy-done.1, f32[2,4,128]{2,1,0:T(4,128)S(1)} %max.29, pred[128,1024]{0,1:T(8,128)(4,1)S(1)} %broadcast_compare_fusion.2, bf16[8192,4,128]{2,0,1:T(8,128)(2,1)} %get-tuple-element.210, s32[]{:T(128)S(6)} %select_n.373, s32[]{:T(128)S(6)} %add.345, ...), kind=kOutput, calls=%fused_computation.8.clone.1 | convolution fusion | flops 273940480 | bytes 5906440 | tf_op jit(solution)/shard_map/while/body/kgqs,skd->kgqd/dot_general | solution.py:130
  232.3 2.0 copy-done.1
  235.4 3.9 %fusion.118 = f32[2,4,128,128]{3,2,1,0:T(8,128)S(1)} fusion(f32[2,1024,4,128]{3,1,2,0:T(8,128)} %copy-done.1, f32[2,4,128]{2,1,0:T(4,128)S(1)} %max.29, pred[128,1024]{0,1:T(8,128)(4,1)S(1)} %broadcast_compare_fusion.2, bf16[8192,4,128]{2,0,1:T(8,128)(2,1)} %get-tuple-element.210, s32[]{:T(128)S(6)} %select_n.373, s32[]{:T(128)S(6)} %add.345, ...), kind=kOutput, calls=%fused_computation.8.clone.1 | convolution fusion | flops 273940480 | bytes 5906440 | tf_op jit(solution)/shard_map/while/body/kgqs,skd->kgqd/dot_general | solution.py:130
  241.3 2.0 copy-done.1
  244.4 3.9 %fusion.118 = f32[2,4,128,128]{3,2,1,0:T(8,128)S(1)} fusion(f32[2,1024,4,128]{3,1,2,0:T(8,128)} %copy-done.1, f32[2,4,128]{2,1,0:T(4,128)S(1)} %max.29, pred[128,1024]{0,1:T(8,128)(4,1)S(1)} %broadcast_compare_fusion.2, bf16[8192,4,128]{2,0,1:T(8,128)(2,1)} %get-tuple-element.210, s32[]{:T(128)S(6)} %select_n.373, s32[]{:T(128)S(6)} %add.345, ...), kind=kOutput, calls=%fused_computation.8.clone.1 | convolution fusion | flops 273940480 | bytes 5906440 | tf_op jit(solution)/shard_map/while/body/kgqs,skd->kgqd/dot_general | solution.py:130
  250.3 2.0 copy-done.1
  253.4 3.9 %fusion.118 = f32[2,4,128,128]{3,2,1,0:T(8,128)S(1)} fusion(f32[2,1024,4,128]{3,1,2,0:T(8,128)} %copy-done.1, f32[2,4,128]{2,1,0:T(4,128)S(1)} %max.29, pred[128,1024]{0,1:T(8,128)(4,1)S(1)} %broadcast_compare_fusion.2, bf16[8192,4,128]{2,0,1:T(8,128)(2,1)} %get-tuple-element.210, s32[]{:T(128)S(6)} %select_n.373, s32[]{:T(128)S(6)} %add.345, ...), kind=kOutput, calls=%fused_computation.8.clone.1 | convolution fusion | flops 273940480 | bytes 5906440 | tf_op jit(solution)/shard_map/while/body/kgqs,skd->kgqd/dot_general | solution.py:130
  (176 shorter events, 74.2 us)
Async XLA Ops:
  6.5 85.8 %copy-start = (bf16[128,16,128]{2,1,0:T(8,128)(2,1)S(1)}, bf16[128,16,128]{2,1,0:T(8,128)(2,1)}, u32[]{:S(2)}) copy-start(bf16[128,16,128]{2,1,0:T(8,128)(2,1)} %param.12) | copy-start | bytes 1572868
  6.5 178.4 %all-gather.2.cloned.1.call-start = ((), (), s32[]{:S(2)}) async-start(), calls=%async_computation | async-start | bytes 8519680 | tf_op jit(solution)/shard_map/all_gather | solution.py:109
  11.2 5.9 %copy-start.15 = (f32[1,32]{1,0:T(1,128)S(1)}, f32[1,32]{1,0:T(1,128)}, u32[]{:S(2)}) copy-start(f32[1,32]{1,0:T(1,128)} %param.18) | copy-start | bytes 388
  11.2 5.9 %copy-start.16 = (f32[1,32]{1,0:T(1,128)S(1)}, f32[1,32]{1,0:T(1,128)}, u32[]{:S(2)}) copy-start(f32[1,32]{1,0:T(1,128)} %param.19) | copy-start | bytes 388
  15.7 4.7 %collective-permute-start = (f32[128,273]{0,1:T(8,128)S(1)}, f32[128,273]{0,1:T(8,128)S(1)}, u32[]{:S(2)}, u32[]{:S(2)}) collective-permute-start(f32[128,273]{0,1:T(8,128)S(1)} %pad_maximum_fusion), channel_id=1, source_target_pairs={{0,1},{1,0},{2,3},{3,2},{4,5},{5,4},{6,7},{7,6},{8,9},{9,8},{10,11... | collective-permute-start | bytes 419336 | tf_op jit(solution)/shard_map/ppermute | solution.py:22
  20.4 111.4 %copy-start.6 = (f32[128,273]{0,1:T(8,128)}, f32[128,273]{0,1:T(8,128)S(1)}, u32[]{:S(2)}) copy-start(f32[128,273]{0,1:T(8,128)S(1)} %fusion.74) | copy-start | bytes 419332
  20.8 36.1 %copy-start.7 = (f32[128,16]{1,0:T(8,128)}, f32[128,16]{1,0:T(8,128)S(1)}, u32[]{:S(2)}) copy-start(f32[128,16]{1,0:T(8,128)S(1)} %reduce_window_sum.11) | copy-start | bytes 24580
  22.2 18.6 %collective-permute-start.6 = (f32[16,64,128]{2,1,0:T(8,128)S(1)}, f32[16,64,128]{2,1,0:T(8,128)}, u32[]{:S(2)}, u32[]{:S(2)}) collective-permute-start(f32[16,64,128]{2,1,0:T(8,128)S(1)} %fusion.76), channel_id=1, source_target_pairs={{0,2},{2,4},{4,6},{6,8},{8,10},{10,12},{12,14},{14,16},{16,18},{18... | collective-permute-start | bytes 1572872 | tf_op jit(solution)/shard_map/ppermute | solution.py:18
  42.0 14.1 %collective-permute-start.7 = (f32[16,64,128]{2,1,0:T(8,128)S(1)}, f32[16,64,128]{2,1,0:T(8,128)S(1)}, u32[]{:S(2)}, u32[]{:S(2)}) collective-permute-start(f32[16,64,128]{2,1,0:T(8,128)S(1)} %multiply_add_fusion.5), channel_id=1, source_target_pairs={{0,4},{2,6},{4,8},{6,10},{8,12},{10,14},{12,16},{14,18},{16,20},{1... | collective-permute-start | bytes 1572872 | tf_op jit(solution)/shard_map/ppermute | solution.py:18
  43.3 11.7 %collective-permute-start.1 = (f32[16]{0:T(128)S(1)}, f32[16]{0:T(128)S(1)}, u32[]{:S(2)}, u32[]{:S(2)}) collective-permute-start(f32[16]{0:T(128)S(1)} %fusion.97), channel_id=1, source_target_pairs={{0,2},{2,4},{4,6},{6,8},{8,10},{10,12},{12,14},{14,16},{16,18},{18... | collective-permute-start | bytes 200 | tf_op jit(solution)/shard_map/ppermute | solution.py:18
  58.1 6.8 %copy-start.2 = (f32[16,64,128]{2,1,0:T(8,128)}, f32[16,64,128]{2,1,0:T(8,128)S(1)}, u32[]{:S(2)}) copy-start(f32[16,64,128]{2,1,0:T(8,128)S(1)} %multiply_add_fusion.4) | copy-start | bytes 1572868
  58.1 31.6 %collective-permute-start.8 = (f32[16,64,128]{2,1,0:T(8,128)S(1)}, f32[16,64,128]{2,1,0:T(8,128)S(1)}, u32[]{:S(2)}, u32[]{:S(2)}) collective-permute-start(f32[16,64,128]{2,1,0:T(8,128)S(1)} %multiply_add_fusion.4), channel_id=1, source_target_pairs={{0,8},{2,10},{4,12},{6,14},{8,16},{10,18},{12,20},{14,22},{16,24},... | collective-permute-start | bytes 1572872 | tf_op jit(solution)/shard_map/ppermute | solution.py:18
  59.4 4.8 %collective-permute-start.2 = (f32[16]{0:T(128)}, f32[16]{0:T(128)S(1)}, u32[]{:S(2)}, u32[]{:S(2)}) collective-permute-start(f32[16]{0:T(128)} %get-tuple-element.95), channel_id=1, source_target_pairs={{0,4},{2,6},{4,8},{6,10},{8,12},{10,14},{12,16},{14,18},{16,20},{1... | collective-permute-start | bytes 200 | tf_op jit(solution)/shard_map/ppermute | solution.py:18
  64.8 24.8 %copy-start.9 = (f32[16]{0:T(128)}, f32[16]{0:T(128)S(1)}, u32[]{:S(2)}) copy-start(f32[16]{0:T(128)S(1)} %fusion.94) | copy-start | bytes 196
  89.7 10.2 %copy-start.4 = (f32[16,64,128]{2,1,0:T(8,128)}, f32[16,64,128]{2,1,0:T(8,128)S(1)}, u32[]{:S(2)}) copy-start(f32[16,64,128]{2,1,0:T(8,128)S(1)} %collective-permute-done.8) | copy-start | bytes 1572868
  91.0 17.2 %collective-permute-start.9 = (f32[16,64,128]{2,1,0:T(8,128)S(1)}, f32[16,64,128]{2,1,0:T(8,128)}, u32[]{:S(2)}, u32[]{:S(2)}) collective-permute-start(f32[16,64,128]{2,1,0:T(8,128)S(1)} %multiply_add_fusion.3), channel_id=1, source_target_pairs={{0,16},{2,18},{4,20},{6,22},{8,24},{10,26},{12,28},{14,30},{16,32}... | collective-permute-start | bytes 1572872 | tf_op jit(solution)/shard_map/ppermute | solution.py:18
  92.4 6.8 %collective-permute-start.3 = (f32[16]{0:T(128)}, f32[16]{0:T(128)S(1)}, u32[]{:S(2)}, u32[]{:S(2)}) collective-permute-start(f32[16]{0:T(128)} %copy-done.9), channel_id=1, source_target_pairs={{0,8},{2,10},{4,12},{6,14},{8,16},{10,18},{12,20},{14,22},{16,24},... | collective-permute-start | bytes 200 | tf_op jit(solution)/shard_map/ppermute | solution.py:18
  99.9 9.5 %copy-start.10 = (f32[16]{0:T(128)}, f32[16]{0:T(128)S(1)}, u32[]{:S(2)}) copy-start(f32[16]{0:T(128)S(1)} %fusion.92) | copy-start | bytes 196
  109.4 50.9 %copy-start.5 = (f32[16,64,128]{2,1,0:T(8,128)S(1)}, f32[16,64,128]{2,1,0:T(8,128)}, u32[]{:S(2)}) copy-start(f32[16,64,128]{2,1,0:T(8,128)} %copy-done.4) | copy-start | bytes 1572868
  109.4 19.0 %collective-permute-start.10 = (f32[16,64,128]{2,1,0:T(8,128)S(1)}, f32[16,64,128]{2,1,0:T(8,128)}, u32[]{:S(2)}, u32[]{:S(2)}) collective-permute-start(f32[16,64,128]{2,1,0:T(8,128)S(1)} %multiply_add_fusion.2), channel_id=1, source_target_pairs={{0,32},{2,34},{4,36},{6,38},{8,40},{10,42},{12,44},{14,46},{16,48}... | collective-permute-start | bytes 1572872 | tf_op jit(solution)/shard_map/ppermute | solution.py:18
  116.0 11.8 %collective-permute-start.4 = (f32[16]{0:T(128)}, f32[16]{0:T(128)}, u32[]{:S(2)}, u32[]{:S(2)}) collective-permute-start(f32[16]{0:T(128)} %copy-done.10), channel_id=1, source_target_pairs={{0,16},{2,18},{4,20},{6,22},{8,24},{10,26},{12,28},{14,30},{16,32}... | collective-permute-start | bytes 200 | tf_op jit(solution)/shard_map/ppermute | solution.py:18
  128.4 4.6 %copy-start.11 = (f32[16]{0:T(128)}, f32[16]{0:T(128)S(1)}, u32[]{:S(2)}) copy-start(f32[16]{0:T(128)S(1)} %fusion.90) | copy-start | bytes 196
  130.5 29.8 %collective-permute-start.11 = (f32[16,64,128]{2,1,0:T(8,128)}, f32[16,64,128]{2,1,0:T(8,128)}, u32[]{:S(2)}, u32[]{:S(2)}) collective-permute-start(f32[16,64,128]{2,1,0:T(8,128)} %multiply_add_fusion.1), channel_id=1, source_target_pairs={{0,64},{2,66},{4,68},{6,70},{8,72},{10,74},{12,76},{14,78},{16,80}... | collective-permute-start | bytes 1572872 | tf_op jit(solution)/shard_map/ppermute | solution.py:18
  136.8 16.5 %collective-permute-start.5 = (f32[16]{0:T(128)}, f32[16]{0:T(128)S(1)}, u32[]{:S(2)}, u32[]{:S(2)}) collective-permute-start(f32[16]{0:T(128)} %copy-done.11), channel_id=1, source_target_pairs={{0,32},{2,34},{4,36},{6,38},{8,40},{10,42},{12,44},{14,46},{16,48}... | collective-permute-start | bytes 200 | tf_op jit(solution)/shard_map/ppermute | solution.py:18
  138.2 46.8 %copy-start.8 = (f32[128,16]{0,1:T(8,128)}, f32[128,16]{0,1:T(8,128)S(1)}, u32[]{:S(2)}) copy-start(f32[128,16]{0,1:T(8,128)S(1)} %copy.54) | copy-start | bytes 24580
  187.3 2.0 copy-start.1
  196.3 2.0 copy-start.1
  205.3 2.0 copy-start.1
  214.3 2.0 copy-start.1
  223.3 2.0 copy-start.1
  232.3 2.0 copy-start.1
  260.7 2.6 collective-permute-start.12
  (6 other events, 6.5 us)
Sparse Core Ops, SparseCore 0:
  10.9 174.0 all-gather.1
